TPU v7x, 256 devices: a whole 4x4x8 slice. The times are simulated.
256 devices in a mesh: rows: 16 (over z, y_hi), bx: 4 (over y_lo, core), by: 4 (over x).
Axes of the slice: x: 4, y: 4 (y_hi: 2, y_lo: 2; y = y_hi * 2 + y_lo), z: 8, core: 2. Of those that a mesh axis runs over, the one named last changes fastest.
Arguments:
- pair_mult: bfloat16 [1048576, 256], P(('rows', 'bx', 'by')), may hold values from -1.5 to 1.5
- pair_dens: float32 [1048576], P(('rows', 'bx', 'by')), may hold values from -3 to 3
- pair_live: int32 [1048576], P(('rows', 'bx', 'by')), may hold values 0 or 1
- pair_box: int32 [1048576], P(('rows', 'bx', 'by')), may hold values from 0 to 767
- inter_mask: int32 [128, 32, 32, 98], P('rows', 'bx', 'by'), may hold values 0 or 1
- row_scale: float32 [98, 256], replicated, may hold values from 0.3 to 1.5
- col_scale: float32 [98, 256], replicated, may hold values from 0.3 to 1.5
- base: bfloat16 [256, 256], replicated, may hold values from -0.0390625 to 0.0390625
- lattice: float32 [256, 256], replicated, may hold values from -0.0009765625 to 0.0009765625
Outputs:
- box_locals: bfloat16 [128, 32, 32, 256], P('rows', 'bx', 'by')
- pair_j: float32 [1048576], P(('rows', 'bx', 'by'))
Inputs may be any that keep to these rules, and one draw needn't show every extreme that they name: `pair_box`: numbers a box of the pair's own x, y slab as (l * 8 + x) * 8 + y with l in 0..11, x in 0..7, y in 0..7, where level l is the box z = (rows index of the device * 8 + l - 2) mod 128.
All inputs are finite; a program needn't handle non-finite values. No bound on the sum of `pair_live` or of `inter_mask` on one device may be relied on, other than what follows from the above.
Results may differ from a plain program's by a relative error of at most 0.007.
Values may be sent and summed in bfloat16 or wider, within the bound.
No kernel may reach another device: no remote copies, remote signals or barrier semaphores. Data moves between devices by JAX's collectives and lax.ppermute only.
A program may use at most 128 MiB of HBM per device.

v0:
```python
import numpy as np
import jax
import jax.numpy as jnp
from jax import lax
from jax.experimental import pallas as pl
from jax.experimental.pallas import tpu as pltpu
from jax.sharding import PartitionSpec as P


def padded_2(x, sides, width):
    for axis, dim in sides:
        count, length = (lax.axis_size(axis), x.shape[dim])
        up = [(i, (i + 1) % count) for i in range(count)]
        down = [(j, i) for i, j in up]
        last = lax.slice_in_dim(x, length - width, length, axis=dim)
        leading = lax.slice_in_dim(x, 0, width, axis=dim)
        before = lax.ppermute(last, axis, up)
        after = lax.ppermute(leading, axis, down)
        x = jnp.concatenate([before, x, after], axis=dim)
    return x


def offset_table():
    listed = []
    for shift_z in range(-2, 3):
        for shift_x in range(-2, 3):
            for shift_y in range(-2, 3):
                if max(abs(shift_z), abs(shift_x), abs(shift_y)) == 2:
                    listed.append((shift_z, shift_x, shift_y))
    return listed


def sum_rounds(axes):
    rounds = []
    for axis in axes:
        count = lax.axis_size(axis)
        stride = 1
        while stride < count:
            group = min(4, count // stride)
            span = stride * group
            shifts = []
            for k in range(1, group):
                pairs = []
                for i in range(count):
                    block, rest = divmod(i, span)
                    pairs.append((i, block * span + (rest + k * stride) % span))
                shifts.append(pairs)
            rounds.append((axis, shifts))
            stride = span
    return rounds


def sum_round(x, step):
    axis, shifts = step
    total = x
    for pairs in shifts:
        total = total + lax.ppermute(x, axis, pairs)
    return total


def far_kernel(tab_ref, pad_ref, mask_ref, rs_ref, cs_ref, base_ref, out_ref, acc_ref, ysh_ref):
    rows = acc_ref.shape[0]
    lanes = mask_ref.shape[1]
    levels = 2
    chunk = levels * 8 * ysh_ref.shape[3]
    acc_ref[...] = jnp.zeros(acc_ref.shape, jnp.float32)
    for c in range(ysh_ref.shape[0]):
        for z in range(ysh_ref.shape[1]):
            ysh_ref[c, z] = pad_ref[z, :, c : c + ysh_ref.shape[3], :]
    lane = lax.broadcasted_iota(jnp.int32, (chunk, lanes), 1)

    def body(o, carry):
        a = tab_ref[3 * o]
        b = tab_ref[3 * o + 1]
        c = tab_ref[3 * o + 2]
        row_scale = rs_ref[pl.ds(o, 1), :]
        col_scale = cs_ref[pl.ds(o, 1), :]
        for q in range(rows // chunk):
            win = ysh_ref[c, pl.ds(a + levels * q, levels), pl.ds(b, 8), :, :].reshape(chunk, -1)
            gate = jnp.sum(
                jnp.where(lane == o, mask_ref[q * chunk : (q + 1) * chunk, :], 0.0), axis=1, keepdims=True
            )
            scaled = (win * gate * row_scale).astype(jnp.bfloat16)
            product = jnp.dot(scaled, base_ref[...], preferred_element_type=jnp.float32)
            acc_ref[q * chunk : (q + 1) * chunk, :] += product * col_scale
        return carry

    lax.fori_loop(0, tab_ref.shape[0] // 3, body, 0, unroll=7)
    out_ref[...] = acc_ref[...]


def far_field(padded, masks, row_scale, col_scale, base):
    rows = masks.shape[0]
    components = base.shape[1]
    table = np.array([[a + 2, b + 2, c + 2] for a, b, c in offset_table()], np.int32).reshape(-1)
    vmem = pltpu.MemorySpace.VMEM if hasattr(pltpu, "MemorySpace") else pltpu.VMEM
    smem = pltpu.MemorySpace.SMEM if hasattr(pltpu, "MemorySpace") else pltpu.SMEM
    return pl.pallas_call(
        far_kernel,
        out_shape=jax.ShapeDtypeStruct((rows, components), jnp.float32),
        in_specs=[pl.BlockSpec(memory_space=smem)] + [pl.BlockSpec(memory_space=vmem)] * 5,
        out_specs=pl.BlockSpec(memory_space=vmem),
        scratch_shapes=[
            pltpu.VMEM((rows, components), jnp.float32),
            pltpu.VMEM((5, padded.shape[0], padded.shape[1], padded.shape[2] - 4, components), jnp.float32),
        ],
        compiler_params=pltpu.CompilerParams(vmem_limit_bytes=48 * 1024 * 1024),
    )(jnp.asarray(table), padded, masks, row_scale, col_scale, base)


def device_body(
    pair_mult, pair_dens, pair_live, pair_box, inter_mask, row_scale, col_scale, base, lattice
):
    components = pair_mult.shape[1]
    depth, width_x, width_y, offsets = inter_mask.shape
    near_boxes = (depth + 4) * width_x * width_y
    weighted = (
        (pair_dens * pair_live.astype(jnp.float32))[:, None] * pair_mult.astype(jnp.float32)
    ).astype(jnp.bfloat16)
    cell_part = jnp.sum(weighted.astype(jnp.float32), 0)
    rounds = sum_rounds(("by", "bx", "rows"))
    cell = sum_round(sum_round(cell_part, rounds[0]), rounds[1])
    labels = lax.iota(jnp.int32, near_boxes)
    selector = (labels[:, None] == pair_box[None, :]).astype(jnp.bfloat16)
    partial_near = jnp.dot(selector, weighted, preferred_element_type=jnp.float32)
    partial_near = partial_near.reshape(depth + 4, width_x, width_y, components)
    count = lax.axis_size("rows")
    up = [(i, (i + 1) % count) for i in range(count)]
    down = [(j, i) for i, j in up]
    from_below = lax.ppermute(partial_near[depth:], "rows", up)
    from_above = lax.ppermute(partial_near[:4], "rows", down)
    zpad = partial_near.at[:4].add(from_below).at[depth:].add(from_above)
    padded = padded_2(zpad, (("bx", 1), ("by", 2)), 2)
    masks = inter_mask.reshape(depth * width_x * width_y, offsets).astype(jnp.float32)
    cell = sum_round(cell, rounds[2])
    far = far_field(padded, masks, row_scale, col_scale, base)
    cell, far, late_mult = lax.optimization_barrier((cell, far, pair_mult))
    near_far = padded_2(far.reshape(depth, width_x, width_y, components), (("rows", 0),), 2)
    cell = sum_round(cell, rounds[3])
    lattice_term = jnp.dot(cell, lattice, precision=lax.Precision.HIGHEST)
    near_locals = (near_far + lattice_term).astype(jnp.bfloat16)
    box_locals = near_locals[2 : 2 + depth]
    flat_locals = near_locals.reshape(near_boxes, components)
    onehot = (pair_box[:, None] == labels[None, :]).astype(jnp.bfloat16)
    picked_rows = jnp.dot(onehot, flat_locals, preferred_element_type=jnp.float32)
    pair_j = jnp.sum(late_mult.astype(jnp.float32) * picked_rows, -1)
    return (box_locals, pair_j)


def solution(mesh):
    return jax.shard_map(
        device_body,
        mesh=mesh,
        in_specs=(
            P(("rows", "bx", "by"), None),
            P(("rows", "bx", "by")),
            P(("rows", "bx", "by")),
            P(("rows", "bx", "by")),
            P("rows", "bx", "by", None),
            P(),
            P(),
            P(),
            P(),
        ),
        out_specs=(P("rows", "bx", "by", None), P(("rows", "bx", "by"))),
        check_vma=False,
    )
```

profile of v0, /device:TPU:6, one launch (start us, length us, event | category | flops | bytes accessed | tf_op | source)
XLA Modules:
  0.0 85.8 jit_solution(15240909786888258334)
XLA Ops:
  0.6 0.0 copy-start
  0.6 0.8 convert_multiply_fusion
  1.4 4.2 %fusion = f32[768,256]{1,0:T(8,128)S(1)} fusion(s32[4096]{0:T(1024)} %param.17, bf16[4096,256]{1,0:T(8,128)(2,1)} %param.14, f32[4096]{0:T(1024)S(1)} %convert_multiply_fusion), kind=kOutput, calls=%fused_computation.2 | convolution fusion | flops 1616904192 | bytes 2916352 | tf_op jit(solution)/shard_map/dot_general | solution.py:125
  5.7 3.3 %collective-permute-start.9 = (f32[4,8,8,256]{3,2,1,0:T(8,128)S(1)}, f32[4,8,8,256]{3,2,1,0:T(8,128)S(1)}, u32[]{:S(2)}, u32[]{:S(2)}) collective-permute-start(f32[4,8,8,256]{3,2,1,0:T(8,128)S(1)} %bitcast.21), channel_id=1, source_target_pairs={{0,16},{16,32},{32,48},{48,64},{64,80},{80,96},{96,112},{112,128},... | collective-permute-start | bytes 786440 | tf_op jit(solution)/shard_map/ppermute | solution.py:130
  8.9 5.4 %collective-permute-start.10 = (f32[4,8,8,256]{3,2,1,0:T(8,128)S(1)}, f32[4,8,8,256]{3,2,1,0:T(8,128)S(1)}, u32[]{:S(2)}, u32[]{:S(2)}) collective-permute-start(f32[4,8,8,256]{3,2,1,0:T(8,128)S(1)} %bitcast.19), channel_id=1, source_target_pairs={{16,0},{32,16},{48,32},{64,48},{80,64},{96,80},{112,96},{128,112},... | collective-permute-start | bytes 786440 | tf_op jit(solution)/shard_map/ppermute | solution.py:131
  14.3 0.0 copy-done.5
  14.3 0.7 convert_reduce_fusion
  15.0 0.0 copy-start.7
  15.0 0.9 %collective-permute-start.2 = (f32[256]{0:T(256)S(1)}, f32[256]{0:T(256)S(1)}, u32[]{:S(2)}, u32[]{:S(2)}) collective-permute-start(f32[256]{0:T(256)S(1)} %convert_reduce_fusion), channel_id=1, source_target_pairs={{0,3},{1,0},{2,1},{3,2},{4,7},{5,4},{6,5},{7,6},{8,11},{9,8},{10,9... | collective-permute-start | bytes 3080 | tf_op jit(solution)/shard_map/ppermute | solution.py:57
  16.0 1.1 %collective-permute-start.1 = (f32[256]{0:T(256)S(1)}, f32[256]{0:T(256)S(1)}, u32[]{:S(2)}, u32[]{:S(2)}) collective-permute-start(f32[256]{0:T(256)S(1)} %convert_reduce_fusion), channel_id=1, source_target_pairs={{0,2},{1,3},{2,0},{3,1},{4,6},{5,7},{6,4},{7,5},{8,10},{9,11},{10,... | collective-permute-start | bytes 3080 | tf_op jit(solution)/shard_map/ppermute | solution.py:57
  17.1 2.1 %collective-permute-start = (f32[256]{0:T(256)S(1)}, f32[256]{0:T(256)S(1)}, u32[]{:S(2)}, u32[]{:S(2)}) collective-permute-start(f32[256]{0:T(256)S(1)} %convert_reduce_fusion), channel_id=1, source_target_pairs={{0,1},{1,2},{2,3},{3,0},{4,5},{5,6},{6,7},{7,4},{8,9},{9,10},{10,1... | collective-permute-start | bytes 3080 | tf_op jit(solution)/shard_map/ppermute | solution.py:57
  19.2 1.5 %collective-permute-done.9 = f32[4,8,8,256]{3,2,1,0:T(8,128)S(1)} collective-permute-done((f32[4,8,8,256]{3,2,1,0:T(8,128)S(1)}, f32[4,8,8,256]{3,2,1,0:T(8,128)S(1)}, u32[]{:S(2)}, u32[]{:S(2)}) %collective-permute-start.9) | collective-permute-done | bytes 262176 | tf_op jit(solution)/shard_map/ppermute | solution.py:130
  20.7 3.1 %collective-permute-done.10 = f32[4,8,8,256]{3,2,1,0:T(8,128)S(1)} collective-permute-done((f32[4,8,8,256]{3,2,1,0:T(8,128)S(1)}, f32[4,8,8,256]{3,2,1,0:T(8,128)S(1)}, u32[]{:S(2)}, u32[]{:S(2)}) %collective-permute-start.10) | collective-permute-done | bytes 262176 | tf_op jit(solution)/shard_map/ppermute | solution.py:131
  23.8 0.1 fusion.8
  23.9 0.1 collective-permute-start.12
  24.0 0.5 collective-permute-start.11
  24.5 0.0 collective-permute-done.2
  24.5 0.0 collective-permute-done.1
  24.5 0.0 collective-permute-done
  24.5 1.4 %collective-permute-start.5 = (f32[256]{0:T(256)S(1)}, f32[256]{0:T(256)S(1)}, u32[]{:S(2)}, u32[]{:S(2)}) collective-permute-start(f32[256]{0:T(256)S(1)} %add_add_fusion.3), channel_id=1, source_target_pairs={{0,12},{4,0},{8,4},{12,8},{1,13},{5,1},{9,5},{13,9},{2,14},{6,2},{... | collective-permute-start | bytes 3080 | tf_op jit(solution)/shard_map/ppermute | solution.py:57
  26.0 0.7 collective-permute-start.4
  26.6 0.0 collective-permute-start.3
  26.6 2.5 %collective-permute-done.12 = f32[12,2,8,256]{3,2,1,0:T(8,128)S(1)} collective-permute-done((f32[12,2,8,256]{3,2,1,0:T(8,128)S(1)}, f32[12,2,8,256]{3,2,1,0:T(8,128)S(1)}, u32[]{:S(2)}, u32[]{:S(2)}) %collective-permute-start.12) | collective-permute-done | bytes 196640 | tf_op jit(solution)/shard_map/ppermute | solution.py:18
  29.1 1.3 %collective-permute-done.11 = f32[12,2,8,256]{3,2,1,0:T(8,128)S(1)} collective-permute-done((f32[12,2,8,256]{3,2,1,0:T(8,128)S(1)}, f32[12,2,8,256]{3,2,1,0:T(8,128)S(1)}, u32[]{:S(2)}, u32[]{:S(2)}) %collective-permute-start.11) | collective-permute-done | bytes 196640 | tf_op jit(solution)/shard_map/ppermute | solution.py:17
  30.5 0.2 pad_maximum_fusion.4
  30.6 0.0 copy-start.1
  30.7 0.0 copy-start.2
  30.7 0.0 copy-start.3
  30.7 0.0 copy-start.4
  30.7 0.9 %collective-permute-start.14 = (f32[12,12,2,256]{3,2,1,0:T(2,128)S(1)}, f32[12,12,2,256]{3,2,1,0:T(2,128)S(1)}, u32[]{:S(2)}, u32[]{:S(2)}) collective-permute-start(f32[12,12,2,256]{3,2,1,0:T(2,128)S(1)} %get-tuple-element.33), channel_id=1, source_target_pairs={{1,0},{2,1},{3,2},{0,3},{5,4},{6,5},{7,6},{4,7},{9,8},{10,9},{11,1... | collective-permute-start | bytes 884744 | tf_op jit(solution)/shard_map/ppermute | solution.py:18
  31.6 2.4 %collective-permute-start.13 = (f32[12,12,2,256]{3,2,1,0:T(2,128)S(1)}, f32[12,12,2,256]{3,2,1,0:T(2,128)S(1)}, u32[]{:S(2)}, u32[]{:S(2)}) collective-permute-start(f32[12,12,2,256]{3,2,1,0:T(2,128)S(1)} %get-tuple-element.32), channel_id=1, source_target_pairs={{0,1},{1,2},{2,3},{3,0},{4,5},{5,6},{6,7},{7,4},{8,9},{9,10},{10,1... | collective-permute-start | bytes 884744 | tf_op jit(solution)/shard_map/ppermute | solution.py:17
  34.0 0.0 collective-permute-done.5
  34.0 0.0 collective-permute-done.4
  34.0 0.0 collective-permute-done.3
  34.0 2.6 %collective-permute-start.8 = (f32[256]{0:T(256)S(1)}, f32[256]{0:T(256)S(1)}, u32[]{:S(2)}, u32[]{:S(2)}) collective-permute-start(f32[256]{0:T(256)S(1)} %add_add_fusion.2), channel_id=1, source_target_pairs={{0,48},{16,0},{32,16},{48,32},{64,112},{80,64},{96,80},{112,96},{1... | collective-permute-start | bytes 3080 | tf_op jit(solution)/shard_map/ppermute | solution.py:57
  36.6 0.1 collective-permute-start.7
  36.7 2.0 %collective-permute-start.6 = (f32[256]{0:T(256)S(1)}, f32[256]{0:T(256)S(1)}, u32[]{:S(2)}, u32[]{:S(2)}) collective-permute-start(f32[256]{0:T(256)S(1)} %add_add_fusion.2), channel_id=1, source_target_pairs={{0,16},{16,32},{32,48},{48,0},{64,80},{80,96},{96,112},{112,64},{1... | collective-permute-start | bytes 3080 | tf_op jit(solution)/shard_map/ppermute | solution.py:57
  38.7 0.7 collective-permute-done.8
  39.4 0.8 collective-permute-done.7
  40.2 2.5 %collective-permute-done.6 = f32[256]{0:T(256)S(1)} collective-permute-done((f32[256]{0:T(256)S(1)}, f32[256]{0:T(256)S(1)}, u32[]{:S(2)}, u32[]{:S(2)}) %collective-permute-start.6) | collective-permute-done | bytes 1056 | tf_op jit(solution)/shard_map/ppermute | solution.py:57
  42.7 0.0 collective-permute-done.14
  42.7 0.0 collective-permute-done.13
  42.7 0.5 pad_maximum_fusion.pad_ref
  43.2 0.0 copy-done.1
  43.2 0.0 copy-done.2
  43.2 0.0 copy-done.3
  43.2 0.0 copy-done.4
  43.2 16.8 %shard_map.113 = f32[512,256]{1,0:T(8,128)S(1)} custom-call(s32[294]{0:T(512)S(1)} %copy-done.4, f32[12,12,12,256]{3,2,1,0:T(8,128)S(1)} %pad_maximum_fusion.pad_ref, f32[512,98]{1,0:T(8,128)S(1)} %bitcast.17, f32[98,256]{1,0:T(8,128)S(1)} %copy-done.2, f32[98,256]{1,0:T(8,128)S(1)} %copy-done.3, bf16[256,256]{1,0:T(8,128)(2,1)S(1)} %copy-done.1), custom_call_target="tpu_custom_call" | custom-call | tf_op jit(solution)/shard_map/pallas_call | solution.py:98
  60.0 6.4 %collective-permute-start.19 = (f32[256]{0:T(256)S(1)}, f32[256]{0:T(256)S(1)}, u32[]{:S(2)}, u32[]{:S(2)}) collective-permute-start(f32[256]{0:T(256)S(1)} %add_add_fusion.1), channel_id=1, source_target_pairs={{0,192},{16,208},{32,224},{48,240},{64,0},{80,16},{96,32},{112,48}... | collective-permute-start | bytes 3080 | tf_op jit(solution)/shard_map/ppermute | solution.py:57
  66.4 1.0 %collective-permute-start.18 = (f32[256]{0:T(256)S(1)}, f32[256]{0:T(256)S(1)}, u32[]{:S(2)}, u32[]{:S(2)}) collective-permute-start(f32[256]{0:T(256)S(1)} %add_add_fusion.1), channel_id=1, source_target_pairs={{0,128},{16,144},{32,160},{48,176},{64,192},{80,208},{96,224},{112... | collective-permute-start | bytes 3080 | tf_op jit(solution)/shard_map/ppermute | solution.py:57
  67.4 2.8 %collective-permute-start.17 = (f32[256]{0:T(256)S(1)}, f32[256]{0:T(256)S(1)}, u32[]{:S(2)}, u32[]{:S(2)}) collective-permute-start(f32[256]{0:T(256)S(1)} %add_add_fusion.1), channel_id=1, source_target_pairs={{0,64},{16,80},{32,96},{48,112},{64,128},{80,144},{96,160},{112,17... | collective-permute-start | bytes 3080 | tf_op jit(solution)/shard_map/ppermute | solution.py:57
  70.3 1.8 %collective-permute-start.16 = (f32[2,8,8,256]{3,2,1,0:T(8,128)S(1)}, f32[2,8,8,256]{3,2,1,0:T(8,128)S(1)}, u32[]{:S(2)}, u32[]{:S(2)}) collective-permute-start(f32[2,8,8,256]{3,2,1,0:T(8,128)S(1)} %bitcast.23), channel_id=1, source_target_pairs={{16,0},{32,16},{48,32},{64,48},{80,64},{96,80},{112,96},{128,112},... | collective-permute-start | bytes 393224 | tf_op jit(solution)/shard_map/ppermute | solution.py:18
  72.0 1.8 %collective-permute-start.15 = (f32[2,8,8,256]{3,2,1,0:T(8,128)S(1)}, f32[2,8,8,256]{3,2,1,0:T(8,128)S(1)}, u32[]{:S(2)}, u32[]{:S(2)}) collective-permute-start(f32[2,8,8,256]{3,2,1,0:T(8,128)S(1)} %bitcast.22), channel_id=1, source_target_pairs={{0,16},{16,32},{32,48},{48,64},{64,80},{80,96},{96,112},{112,128},... | collective-permute-start | bytes 393224 | tf_op jit(solution)/shard_map/ppermute | solution.py:17
  73.9 3.0 %copy.12 = bf16[4096,256]{0,1:T(8,128)(2,1)} copy(bf16[4096,256]{1,0:T(8,128)(2,1)S(1)} %copy-done.5) | data formatting | bytes 4194304 | tf_op jit(solution)/shard_map/optimization_barrier | solution.py:137
  76.8 0.0 collective-permute-done.19
  76.8 0.0 collective-permute-done.18
  76.8 0.0 collective-permute-done.17
  76.9 0.2 fusion.12
  77.1 0.5 collective-permute-done.16
  77.5 3.1 %collective-permute-done.15 = f32[2,8,8,256]{3,2,1,0:T(8,128)S(1)} collective-permute-done((f32[2,8,8,256]{3,2,1,0:T(8,128)S(1)}, f32[2,8,8,256]{3,2,1,0:T(8,128)S(1)}, u32[]{:S(2)}, u32[]{:S(2)}) %collective-permute-start.15) | collective-permute-done | bytes 131104 | tf_op jit(solution)/shard_map/ppermute | solution.py:17
  80.6 0.1 pad_maximum_fusion.1
  80.7 0.7 fusion.7
  81.4 0.1 fusion.6
  81.5 4.3 %fusion.5 = f32[4096]{0:T(1024)} fusion(bf16[768,256]{1,0:T(8,128)(2,1)S(1)} %fusion.6, s32[4096]{0:T(1024)S(1)} %copy-done.8, bf16[4096,256]{0,1:T(8,128)(2,1)S(1)} %copy-done.6), kind=kOutput, calls=%fused_computation.10 | convolution fusion | flops 1616900096 | bytes 2523136 | tf_op jit(solution)/shard_map/dot_general | solution.py:145
  (16 shorter events, 0.2 us)
Async XLA Ops:
  0.6 76.2 %copy-start = (f32[256,256]{1,0:T(8,128)S(1)}, f32[256,256]{1,0:T(8,128)}, u32[]{:S(2)}) copy-start(f32[256,256]{1,0:T(8,128)} %param.22) | copy-start | bytes 786436
  1.4 12.9 %copy-start.5 = (bf16[4096,256]{1,0:T(8,128)(2,1)S(1)}, bf16[4096,256]{1,0:T(8,128)(2,1)}, u32[]{:S(2)}) copy-start(bf16[4096,256]{1,0:T(8,128)(2,1)} %param.14) | copy-start | bytes 6291460
  5.7 15.0 %collective-permute-start.9 = (f32[4,8,8,256]{3,2,1,0:T(8,128)S(1)}, f32[4,8,8,256]{3,2,1,0:T(8,128)S(1)}, u32[]{:S(2)}, u32[]{:S(2)}) collective-permute-start(f32[4,8,8,256]{3,2,1,0:T(8,128)S(1)} %bitcast.21), channel_id=1, source_target_pairs={{0,16},{16,32},{32,48},{48,64},{64,80},{80,96},{96,112},{112,128},... | collective-permute-start | bytes 786440 | tf_op jit(solution)/shard_map/ppermute | solution.py:130
  8.9 14.9 %collective-permute-start.10 = (f32[4,8,8,256]{3,2,1,0:T(8,128)S(1)}, f32[4,8,8,256]{3,2,1,0:T(8,128)S(1)}, u32[]{:S(2)}, u32[]{:S(2)}) collective-permute-start(f32[4,8,8,256]{3,2,1,0:T(8,128)S(1)} %bitcast.19), channel_id=1, source_target_pairs={{16,0},{32,16},{48,32},{64,48},{80,64},{96,80},{112,96},{128,112},... | collective-permute-start | bytes 786440 | tf_op jit(solution)/shard_map/ppermute | solution.py:131
  15.0 23.7 %copy-start.7 = (s32[8,8,8,98]{3,2,1,0:T(8,128)S(1)}, s32[8,8,8,98]{3,2,1,0:T(8,128)}, u32[]{:S(2)}) copy-start(s32[8,8,8,98]{3,2,1,0:T(8,128)} %param.18) | copy-start | bytes 602116
  15.0 9.5 %collective-permute-start.2 = (f32[256]{0:T(256)S(1)}, f32[256]{0:T(256)S(1)}, u32[]{:S(2)}, u32[]{:S(2)}) collective-permute-start(f32[256]{0:T(256)S(1)} %convert_reduce_fusion), channel_id=1, source_target_pairs={{0,3},{1,0},{2,1},{3,2},{4,7},{5,4},{6,5},{7,6},{8,11},{9,8},{10,9... | collective-permute-start | bytes 3080 | tf_op jit(solution)/shard_map/ppermute | solution.py:57
  16.0 8.6 %collective-permute-start.1 = (f32[256]{0:T(256)S(1)}, f32[256]{0:T(256)S(1)}, u32[]{:S(2)}, u32[]{:S(2)}) collective-permute-start(f32[256]{0:T(256)S(1)} %convert_reduce_fusion), channel_id=1, source_target_pairs={{0,2},{1,3},{2,0},{3,1},{4,6},{5,7},{6,4},{7,5},{8,10},{9,11},{10,... | collective-permute-start | bytes 3080 | tf_op jit(solution)/shard_map/ppermute | solution.py:57
  17.1 7.5 %collective-permute-start = (f32[256]{0:T(256)S(1)}, f32[256]{0:T(256)S(1)}, u32[]{:S(2)}, u32[]{:S(2)}) collective-permute-start(f32[256]{0:T(256)S(1)} %convert_reduce_fusion), channel_id=1, source_target_pairs={{0,1},{1,2},{2,3},{3,0},{4,5},{5,6},{6,7},{7,4},{8,9},{9,10},{10,1... | collective-permute-start | bytes 3080 | tf_op jit(solution)/shard_map/ppermute | solution.py:57
  23.9 5.2 %collective-permute-start.12 = (f32[12,2,8,256]{3,2,1,0:T(8,128)S(1)}, f32[12,2,8,256]{3,2,1,0:T(8,128)S(1)}, u32[]{:S(2)}, u32[]{:S(2)}) collective-permute-start(f32[12,2,8,256]{3,2,1,0:T(8,128)S(1)} %get-tuple-element.35), channel_id=1, source_target_pairs={{4,0},{8,4},{12,8},{0,12},{5,1},{9,5},{13,9},{1,13},{6,2},{10,6},{... | collective-permute-start | bytes 589832 | tf_op jit(solution)/shard_map/ppermute | solution.py:18
  24.0 6.4 %collective-permute-start.11 = (f32[12,2,8,256]{3,2,1,0:T(8,128)S(1)}, f32[12,2,8,256]{3,2,1,0:T(8,128)S(1)}, u32[]{:S(2)}, u32[]{:S(2)}) collective-permute-start(f32[12,2,8,256]{3,2,1,0:T(8,128)S(1)} %get-tuple-element.34), channel_id=1, source_target_pairs={{0,4},{4,8},{8,12},{12,0},{1,5},{5,9},{9,13},{13,1},{2,6},{6,10},{... | collective-permute-start | bytes 589832 | tf_op jit(solution)/shard_map/ppermute | solution.py:17
  24.5 9.5 %collective-permute-start.5 = (f32[256]{0:T(256)S(1)}, f32[256]{0:T(256)S(1)}, u32[]{:S(2)}, u32[]{:S(2)}) collective-permute-start(f32[256]{0:T(256)S(1)} %add_add_fusion.3), channel_id=1, source_target_pairs={{0,12},{4,0},{8,4},{12,8},{1,13},{5,1},{9,5},{13,9},{2,14},{6,2},{... | collective-permute-start | bytes 3080 | tf_op jit(solution)/shard_map/ppermute | solution.py:57
  26.0 8.1 %collective-permute-start.4 = (f32[256]{0:T(256)S(1)}, f32[256]{0:T(256)S(1)}, u32[]{:S(2)}, u32[]{:S(2)}) collective-permute-start(f32[256]{0:T(256)S(1)} %add_add_fusion.3), channel_id=1, source_target_pairs={{0,8},{4,12},{8,0},{12,4},{1,9},{5,13},{9,1},{13,5},{2,10},{6,14},... | collective-permute-start | bytes 3080 | tf_op jit(solution)/shard_map/ppermute | solution.py:57
  26.6 7.4 %collective-permute-start.3 = (f32[256]{0:T(256)S(1)}, f32[256]{0:T(256)S(1)}, u32[]{:S(2)}, u32[]{:S(2)}) collective-permute-start(f32[256]{0:T(256)S(1)} %add_add_fusion.3), channel_id=1, source_target_pairs={{0,4},{4,8},{8,12},{12,0},{1,5},{5,9},{9,13},{13,1},{2,6},{6,10},{... | collective-permute-start | bytes 3080 | tf_op jit(solution)/shard_map/ppermute | solution.py:57
  30.6 12.5 %copy-start.1 = (bf16[256,256]{1,0:T(8,128)(2,1)S(1)}, bf16[256,256]{1,0:T(8,128)(2,1)}, u32[]{:S(2)}) copy-start(bf16[256,256]{1,0:T(8,128)(2,1)} %base_ref.1) | copy-start | bytes 393220
  30.7 12.5 %copy-start.2 = (f32[98,256]{1,0:T(8,128)S(1)}, f32[98,256]{1,0:T(8,128)}, u32[]{:S(2)}) copy-start(f32[98,256]{1,0:T(8,128)} %rs_ref.1) | copy-start | bytes 301060
  30.7 12.5 %copy-start.3 = (f32[98,256]{1,0:T(8,128)S(1)}, f32[98,256]{1,0:T(8,128)}, u32[]{:S(2)}) copy-start(f32[98,256]{1,0:T(8,128)} %cs_ref.1) | copy-start | bytes 301060
  30.7 12.5 %copy-start.4 = (s32[294]{0:T(512)S(1)}, s32[294]{0:T(512)}, u32[]{:S(2)}) copy-start(s32[294]{0:T(512)} %constant.59.clone.tab_ref) | copy-start | bytes 3532
  30.7 12.0 %collective-permute-start.14 = (f32[12,12,2,256]{3,2,1,0:T(2,128)S(1)}, f32[12,12,2,256]{3,2,1,0:T(2,128)S(1)}, u32[]{:S(2)}, u32[]{:S(2)}) collective-permute-start(f32[12,12,2,256]{3,2,1,0:T(2,128)S(1)} %get-tuple-element.33), channel_id=1, source_target_pairs={{1,0},{2,1},{3,2},{0,3},{5,4},{6,5},{7,6},{4,7},{9,8},{10,9},{11,1... | collective-permute-start | bytes 884744 | tf_op jit(solution)/shard_map/ppermute | solution.py:18
  31.6 11.1 %collective-permute-start.13 = (f32[12,12,2,256]{3,2,1,0:T(2,128)S(1)}, f32[12,12,2,256]{3,2,1,0:T(2,128)S(1)}, u32[]{:S(2)}, u32[]{:S(2)}) collective-permute-start(f32[12,12,2,256]{3,2,1,0:T(2,128)S(1)} %get-tuple-element.32), channel_id=1, source_target_pairs={{0,1},{1,2},{2,3},{3,0},{4,5},{5,6},{6,7},{7,4},{8,9},{9,10},{10,1... | collective-permute-start | bytes 884744 | tf_op jit(solution)/shard_map/ppermute | solution.py:17
  34.0 5.3 %collective-permute-start.8 = (f32[256]{0:T(256)S(1)}, f32[256]{0:T(256)S(1)}, u32[]{:S(2)}, u32[]{:S(2)}) collective-permute-start(f32[256]{0:T(256)S(1)} %add_add_fusion.2), channel_id=1, source_target_pairs={{0,48},{16,0},{32,16},{48,32},{64,112},{80,64},{96,80},{112,96},{1... | collective-permute-start | bytes 3080 | tf_op jit(solution)/shard_map/ppermute | solution.py:57
  36.6 3.6 %collective-permute-start.7 = (f32[256]{0:T(256)S(1)}, f32[256]{0:T(256)S(1)}, u32[]{:S(2)}, u32[]{:S(2)}) collective-permute-start(f32[256]{0:T(256)S(1)} %add_add_fusion.2), channel_id=1, source_target_pairs={{0,32},{16,48},{32,0},{48,16},{64,96},{80,112},{96,64},{112,80},{1... | collective-permute-start | bytes 3080 | tf_op jit(solution)/shard_map/ppermute | solution.py:57
  36.7 6.0 %collective-permute-start.6 = (f32[256]{0:T(256)S(1)}, f32[256]{0:T(256)S(1)}, u32[]{:S(2)}, u32[]{:S(2)}) collective-permute-start(f32[256]{0:T(256)S(1)} %add_add_fusion.2), channel_id=1, source_target_pairs={{0,16},{16,32},{32,48},{48,0},{64,80},{80,96},{96,112},{112,64},{1... | collective-permute-start | bytes 3080 | tf_op jit(solution)/shard_map/ppermute | solution.py:57
  60.0 16.8 %collective-permute-start.19 = (f32[256]{0:T(256)S(1)}, f32[256]{0:T(256)S(1)}, u32[]{:S(2)}, u32[]{:S(2)}) collective-permute-start(f32[256]{0:T(256)S(1)} %add_add_fusion.1), channel_id=1, source_target_pairs={{0,192},{16,208},{32,224},{48,240},{64,0},{80,16},{96,32},{112,48}... | collective-permute-start | bytes 3080 | tf_op jit(solution)/shard_map/ppermute | solution.py:57
  66.4 10.4 %collective-permute-start.18 = (f32[256]{0:T(256)S(1)}, f32[256]{0:T(256)S(1)}, u32[]{:S(2)}, u32[]{:S(2)}) collective-permute-start(f32[256]{0:T(256)S(1)} %add_add_fusion.1), channel_id=1, source_target_pairs={{0,128},{16,144},{32,160},{48,176},{64,192},{80,208},{96,224},{112... | collective-permute-start | bytes 3080 | tf_op jit(solution)/shard_map/ppermute | solution.py:57
  67.4 9.4 %collective-permute-start.17 = (f32[256]{0:T(256)S(1)}, f32[256]{0:T(256)S(1)}, u32[]{:S(2)}, u32[]{:S(2)}) collective-permute-start(f32[256]{0:T(256)S(1)} %add_add_fusion.1), channel_id=1, source_target_pairs={{0,64},{16,80},{32,96},{48,112},{64,128},{80,144},{96,160},{112,17... | collective-permute-start | bytes 3080 | tf_op jit(solution)/shard_map/ppermute | solution.py:57
  70.3 7.3 %collective-permute-start.16 = (f32[2,8,8,256]{3,2,1,0:T(8,128)S(1)}, f32[2,8,8,256]{3,2,1,0:T(8,128)S(1)}, u32[]{:S(2)}, u32[]{:S(2)}) collective-permute-start(f32[2,8,8,256]{3,2,1,0:T(8,128)S(1)} %bitcast.23), channel_id=1, source_target_pairs={{16,0},{32,16},{48,32},{64,48},{80,64},{96,80},{112,96},{128,112},... | collective-permute-start | bytes 393224 | tf_op jit(solution)/shard_map/ppermute | solution.py:18
  72.0 8.6 %collective-permute-start.15 = (f32[2,8,8,256]{3,2,1,0:T(8,128)S(1)}, f32[2,8,8,256]{3,2,1,0:T(8,128)S(1)}, u32[]{:S(2)}, u32[]{:S(2)}) collective-permute-start(f32[2,8,8,256]{3,2,1,0:T(8,128)S(1)} %bitcast.22), channel_id=1, source_target_pairs={{0,16},{16,32},{32,48},{48,64},{64,80},{80,96},{96,112},{112,128},... | collective-permute-start | bytes 393224 | tf_op jit(solution)/shard_map/ppermute | solution.py:17
  76.8 4.7 %copy-start.6 = (bf16[4096,256]{0,1:T(8,128)(2,1)S(1)}, bf16[4096,256]{0,1:T(8,128)(2,1)}, u32[]{:S(2)}) copy-start(bf16[4096,256]{0,1:T(8,128)(2,1)} %copy.12) | copy-start | bytes 6291460
  76.8 4.7 %copy-start.8 = (s32[4096]{0:T(1024)S(1)}, s32[4096]{0:T(1024)}, u32[]{:S(2)}) copy-start(s32[4096]{0:T(1024)} %param.17) | copy-start | bytes 49156
where the time goes:
time: 86 us; the launch traced here: 85.8 us
  starting transfers between devices  37.2 us (43%)
  Pallas kernels  16.8 us (20%)
  waiting for transfers between devices  16 us (19%)
  matrix products  8.69 us (10%)
  other arithmetic  3.14 us (4%)
  local copies, waits for them, and re-layouts  3.1 us (4%)
  between operations  0.88 us (1%)
    ppermute x12, starting transfers between devices, sum_round(): total = total + lax.ppermute(x, axis, pairs)  21 us
    pallas_call x1, Pallas kernels, far_field(): pl.pallas_call(far_kernel, out_shape=jax.ShapeDtypeStruct((rows, componen...  16.8 us
    ppermute x1, starting transfers between devices, device_body(): from_above = lax.ppermute(partial_near[:4], 'rows', down)  5.38 us
    ppermute x3, starting transfers between devices, padded_2(): before = lax.ppermute(last, axis, up)  4.74 us
    ppermute x3, waiting for transfers between devices, padded_2(): before = lax.ppermute(last, axis, up)  4.44 us
    dot_general x1, matrix products, device_body(): jnp.dot(onehot, flat_locals, preferred_element_type=jnp.float32)  4.31 us
    dot_general x1, matrix products, device_body(): jnp.dot(selector, weighted, preferred_element_type=jnp.float32)  4.19 us
    ppermute x12, waiting for transfers between devices, sum_round(): total = total + lax.ppermute(x, axis, pairs)  3.98 us
  transfers between devices with their start and end apart: 20, of which 9 were waited for; matrix products, arithmetic and copies ran while one was open for 5% of the time, Pallas kernels for 0%

commit v1 on v0

--- a/solution.py
+++ b/solution.py
@@ -61,7 +61,7 @@
 def far_kernel(tab_ref, pad_ref, mask_ref, rs_ref, cs_ref, base_ref, out_ref, acc_ref, ysh_ref):
     rows = acc_ref.shape[0]
     lanes = mask_ref.shape[1]
-    levels = 2
+    levels = 8
     chunk = levels * 8 * ysh_ref.shape[3]
     acc_ref[...] = jnp.zeros(acc_ref.shape, jnp.float32)
     for c in range(ysh_ref.shape[0]):
@@ -85,7 +85,7 @@
             acc_ref[q * chunk : (q + 1) * chunk, :] += product * col_scale
         return carry
 
-    lax.fori_loop(0, tab_ref.shape[0] // 3, body, 0, unroll=7)
+    lax.fori_loop(0, tab_ref.shape[0] // 3, body, 0, unroll=14)
     out_ref[...] = acc_ref[...]
 
 
@@ -134,7 +134,7 @@
     masks = inter_mask.reshape(depth * width_x * width_y, offsets).astype(jnp.float32)
     cell = sum_round(cell, rounds[2])
     far = far_field(padded, masks, row_scale, col_scale, base)
-    cell, far, late_mult = lax.optimization_barrier((cell, far, pair_mult))
+    cell, far = lax.optimization_barrier((cell, far))
     near_far = padded_2(far.reshape(depth, width_x, width_y, components), (("rows", 0),), 2)
     cell = sum_round(cell, rounds[3])
     lattice_term = jnp.dot(cell, lattice, precision=lax.Precision.HIGHEST)
@@ -143,7 +143,7 @@
     flat_locals = near_locals.reshape(near_boxes, components)
     onehot = (pair_box[:, None] == labels[None, :]).astype(jnp.bfloat16)
     picked_rows = jnp.dot(onehot, flat_locals, preferred_element_type=jnp.float32)
-    pair_j = jnp.sum(late_mult.astype(jnp.float32) * picked_rows, -1)
+    pair_j = jnp.sum(pair_mult.astype(jnp.float32) * picked_rows, -1)
     return (box_locals, pair_j)
 
 

time: 86 us -> 83 us (0.965)
  Pallas kernels: 16.8 us -> 13.6 us
  waiting for transfers between devices: 16 us -> 19.2 us
  matrix products: 8.69 us -> 6.83 us
  other arithmetic: 3.14 us -> 2.16 us
    pallas_call x1, Pallas kernels: 16.8 us -> 13.6 us  [far_field(): pl.pallas_call(far_kernel, out_shape=jax.ShapeDtypeStruct((rows, componen...]
    optimization_barrier x1 -> x0, local copies, waits for them, and re-layouts: 2.97 us -> none  [device_body(): cell, far, late_mult = lax.optimization_barrier((cell, far, pair_mult))]
    ppermute x3, waiting for transfers between devices: 2.94 us -> 5.91 us  [padded_2(): after = lax.ppermute(leading, axis, down)]
    unnamed x18 -> x19, local copies, waits for them, and re-layouts: 0.05 us -> 3.01 us
    dot_general x1, matrix products: 4.19 us -> 2.39 us  [device_body(): jnp.dot(selector, weighted, preferred_element_type=jnp.float32)]
  transfers between devices with their start and end apart: 20 -> 20, of which waited for: 9 -> 9; matrix products, arithmetic and copies ran while one was open for 5% -> 1% of each run, Pallas kernels for 0% -> 0%
where the time goes in v1:
time: 83 us; the launch traced here: 82.8 us
  starting transfers between devices  37 us (45%)
  waiting for transfers between devices  19.2 us (23%)
  Pallas kernels  13.6 us (16%)
  matrix products  6.83 us (8%)
  local copies, waits for them, and re-layouts  3.09 us (4%)
  other arithmetic  2.16 us (3%)
  between operations  0.9 us (1%)
    ppermute x12, starting transfers between devices, sum_round(): total = total + lax.ppermute(x, axis, pairs)  20.9 us
    pallas_call x1, Pallas kernels, far_field(): pl.pallas_call(far_kernel, out_shape=jax.ShapeDtypeStruct((rows, componen...  13.6 us
    ppermute x3, waiting for transfers between devices, padded_2(): after = lax.ppermute(leading, axis, down)  5.91 us
    ppermute x1, starting transfers between devices, device_body(): from_above = lax.ppermute(partial_near[:4], 'rows', down)  5.38 us
    ppermute x3, starting transfers between devices, padded_2(): before = lax.ppermute(last, axis, up)  4.73 us
    ppermute x3, waiting for transfers between devices, padded_2(): before = lax.ppermute(last, axis, up)  4.44 us
    dot_general x1, matrix products, device_body(): jnp.dot(onehot, flat_locals, preferred_element_type=jnp.float32)  4.26 us
    ppermute x12, waiting for transfers between devices, sum_round(): total = total + lax.ppermute(x, axis, pairs)  4 us
  transfers between devices with their start and end apart: 20, of which 9 were waited for; matrix products, arithmetic and copies ran while one was open for 1% of the time, Pallas kernels for 0%

profile of v1, /device:TPU:6, one launch (start us, length us, event | category | flops | bytes accessed | tf_op | source)
XLA Modules:
  0.0 82.8 jit_solution(17755929569261436857)
XLA Ops:
  0.6 0.0 copy-start
  0.6 0.0 copy-start.6
  0.7 0.0 copy-start.7
  0.7 0.0 copy-start.8
  0.7 3.0 %copy.12 = bf16[4096,256]{0,1:T(8,128)(2,1)S(1)} copy(bf16[4096,256]{1,0:T(8,128)(2,1)} %param.14) | data formatting | bytes 4194304 | tf_op args[0]
  3.6 0.0 copy-done.6
  3.7 0.0 copy-done.7
  3.7 0.0 copy-done.8
  3.7 2.4 %fusion = f32[768,256]{1,0:T(8,128)S(1)} fusion(s32[4096]{0:T(1024)S(1)} %copy-done.8, bf16[4096,256]{0,1:T(8,128)(2,1)S(1)} %copy.12, f32[4096]{0:T(1024)S(1)} %convert_multiply_fusion.1), kind=kOutput, calls=%fused_computation.2 | convolution fusion | flops 1616904192 | bytes 2916352 | tf_op jit(solution)/shard_map/dot_general | solution.py:125
  6.1 3.3 %collective-permute-start.9 = (f32[4,8,8,256]{3,2,1,0:T(8,128)S(1)}, f32[4,8,8,256]{3,2,1,0:T(8,128)S(1)}, u32[]{:S(2)}, u32[]{:S(2)}) collective-permute-start(f32[4,8,8,256]{3,2,1,0:T(8,128)S(1)} %bitcast.21), channel_id=1, source_target_pairs={{0,16},{16,32},{32,48},{48,64},{64,80},{80,96},{96,112},{112,128},... | collective-permute-start | bytes 786440 | tf_op jit(solution)/shard_map/ppermute | solution.py:130
  9.4 5.4 %collective-permute-start.10 = (f32[4,8,8,256]{3,2,1,0:T(8,128)S(1)}, f32[4,8,8,256]{3,2,1,0:T(8,128)S(1)}, u32[]{:S(2)}, u32[]{:S(2)}) collective-permute-start(f32[4,8,8,256]{3,2,1,0:T(8,128)S(1)} %bitcast.19), channel_id=1, source_target_pairs={{16,0},{32,16},{48,32},{64,48},{80,64},{96,80},{112,96},{128,112},... | collective-permute-start | bytes 786440 | tf_op jit(solution)/shard_map/ppermute | solution.py:131
  14.8 0.5 convert_reduce_fusion
  15.3 0.9 %collective-permute-start.2 = (f32[256]{0:T(256)S(1)}, f32[256]{0:T(256)S(1)}, u32[]{:S(2)}, u32[]{:S(2)}) collective-permute-start(f32[256]{0:T(256)S(1)} %convert_reduce_fusion), channel_id=1, source_target_pairs={{0,3},{1,0},{2,1},{3,2},{4,7},{5,4},{6,5},{7,6},{8,11},{9,8},{10,9... | collective-permute-start | bytes 3080 | tf_op jit(solution)/shard_map/ppermute | solution.py:57
  16.2 1.1 %collective-permute-start.1 = (f32[256]{0:T(256)S(1)}, f32[256]{0:T(256)S(1)}, u32[]{:S(2)}, u32[]{:S(2)}) collective-permute-start(f32[256]{0:T(256)S(1)} %convert_reduce_fusion), channel_id=1, source_target_pairs={{0,2},{1,3},{2,0},{3,1},{4,6},{5,7},{6,4},{7,5},{8,10},{9,11},{10,... | collective-permute-start | bytes 3080 | tf_op jit(solution)/shard_map/ppermute | solution.py:57
  17.3 2.1 %collective-permute-start = (f32[256]{0:T(256)S(1)}, f32[256]{0:T(256)S(1)}, u32[]{:S(2)}, u32[]{:S(2)}) collective-permute-start(f32[256]{0:T(256)S(1)} %convert_reduce_fusion), channel_id=1, source_target_pairs={{0,1},{1,2},{2,3},{3,0},{4,5},{5,6},{6,7},{7,4},{8,9},{9,10},{10,1... | collective-permute-start | bytes 3080 | tf_op jit(solution)/shard_map/ppermute | solution.py:57
  19.4 1.7 %collective-permute-done.9 = f32[4,8,8,256]{3,2,1,0:T(8,128)S(1)} collective-permute-done((f32[4,8,8,256]{3,2,1,0:T(8,128)S(1)}, f32[4,8,8,256]{3,2,1,0:T(8,128)S(1)}, u32[]{:S(2)}, u32[]{:S(2)}) %collective-permute-start.9) | collective-permute-done | bytes 262176 | tf_op jit(solution)/shard_map/ppermute | solution.py:130
  21.1 3.1 %collective-permute-done.10 = f32[4,8,8,256]{3,2,1,0:T(8,128)S(1)} collective-permute-done((f32[4,8,8,256]{3,2,1,0:T(8,128)S(1)}, f32[4,8,8,256]{3,2,1,0:T(8,128)S(1)}, u32[]{:S(2)}, u32[]{:S(2)}) %collective-permute-start.10) | collective-permute-done | bytes 262176 | tf_op jit(solution)/shard_map/ppermute | solution.py:131
  24.3 0.1 fusion.10
  24.4 0.1 collective-permute-start.12
  24.5 0.5 collective-permute-start.11
  25.0 0.0 collective-permute-done.2
  25.0 0.0 collective-permute-done.1
  25.0 0.0 collective-permute-done
  25.0 1.4 %collective-permute-start.5 = (f32[256]{0:T(256)S(1)}, f32[256]{0:T(256)S(1)}, u32[]{:S(2)}, u32[]{:S(2)}) collective-permute-start(f32[256]{0:T(256)S(1)} %add_add_fusion.3), channel_id=1, source_target_pairs={{0,12},{4,0},{8,4},{12,8},{1,13},{5,1},{9,5},{13,9},{2,14},{6,2},{... | collective-permute-start | bytes 3080 | tf_op jit(solution)/shard_map/ppermute | solution.py:57
  26.4 0.7 collective-permute-start.4
  27.1 0.0 collective-permute-start.3
  27.1 2.5 %collective-permute-done.12 = f32[12,2,8,256]{3,2,1,0:T(8,128)S(1)} collective-permute-done((f32[12,2,8,256]{3,2,1,0:T(8,128)S(1)}, f32[12,2,8,256]{3,2,1,0:T(8,128)S(1)}, u32[]{:S(2)}, u32[]{:S(2)}) %collective-permute-start.12) | collective-permute-done | bytes 196640 | tf_op jit(solution)/shard_map/ppermute | solution.py:18
  29.6 1.3 %collective-permute-done.11 = f32[12,2,8,256]{3,2,1,0:T(8,128)S(1)} collective-permute-done((f32[12,2,8,256]{3,2,1,0:T(8,128)S(1)}, f32[12,2,8,256]{3,2,1,0:T(8,128)S(1)}, u32[]{:S(2)}, u32[]{:S(2)}) %collective-permute-start.11) | collective-permute-done | bytes 196640 | tf_op jit(solution)/shard_map/ppermute | solution.py:17
  30.9 0.2 pad_maximum_fusion.4
  31.1 0.0 copy-start.1
  31.1 0.0 copy-start.2
  31.1 0.0 copy-start.3
  31.1 0.0 copy-start.4
  31.1 0.9 %collective-permute-start.14 = (f32[12,12,2,256]{3,2,1,0:T(2,128)S(1)}, f32[12,12,2,256]{3,2,1,0:T(2,128)S(1)}, u32[]{:S(2)}, u32[]{:S(2)}) collective-permute-start(f32[12,12,2,256]{3,2,1,0:T(2,128)S(1)} %get-tuple-element.31), channel_id=1, source_target_pairs={{1,0},{2,1},{3,2},{0,3},{5,4},{6,5},{7,6},{4,7},{9,8},{10,9},{11,1... | collective-permute-start | bytes 884744 | tf_op jit(solution)/shard_map/ppermute | solution.py:18
  32.1 2.4 %collective-permute-start.13 = (f32[12,12,2,256]{3,2,1,0:T(2,128)S(1)}, f32[12,12,2,256]{3,2,1,0:T(2,128)S(1)}, u32[]{:S(2)}, u32[]{:S(2)}) collective-permute-start(f32[12,12,2,256]{3,2,1,0:T(2,128)S(1)} %get-tuple-element.30), channel_id=1, source_target_pairs={{0,1},{1,2},{2,3},{3,0},{4,5},{5,6},{6,7},{7,4},{8,9},{9,10},{10,1... | collective-permute-start | bytes 884744 | tf_op jit(solution)/shard_map/ppermute | solution.py:17
  34.5 0.0 collective-permute-done.5
  34.5 0.0 collective-permute-done.4
  34.5 0.0 collective-permute-done.3
  34.5 2.4 %collective-permute-start.8 = (f32[256]{0:T(256)S(1)}, f32[256]{0:T(256)S(1)}, u32[]{:S(2)}, u32[]{:S(2)}) collective-permute-start(f32[256]{0:T(256)S(1)} %add_add_fusion.2), channel_id=1, source_target_pairs={{0,48},{16,0},{32,16},{48,32},{64,112},{80,64},{96,80},{112,96},{1... | collective-permute-start | bytes 3080 | tf_op jit(solution)/shard_map/ppermute | solution.py:57
  36.9 0.1 collective-permute-start.7
  37.0 2.0 %collective-permute-start.6 = (f32[256]{0:T(256)S(1)}, f32[256]{0:T(256)S(1)}, u32[]{:S(2)}, u32[]{:S(2)}) collective-permute-start(f32[256]{0:T(256)S(1)} %add_add_fusion.2), channel_id=1, source_target_pairs={{0,16},{16,32},{32,48},{48,0},{64,80},{80,96},{96,112},{112,64},{1... | collective-permute-start | bytes 3080 | tf_op jit(solution)/shard_map/ppermute | solution.py:57
  39.0 0.6 collective-permute-done.8
  39.6 0.8 collective-permute-done.7
  40.4 2.5 %collective-permute-done.6 = f32[256]{0:T(256)S(1)} collective-permute-done((f32[256]{0:T(256)S(1)}, f32[256]{0:T(256)S(1)}, u32[]{:S(2)}, u32[]{:S(2)}) %collective-permute-start.6) | collective-permute-done | bytes 1056 | tf_op jit(solution)/shard_map/ppermute | solution.py:57
  42.9 0.0 collective-permute-done.14
  43.0 0.0 collective-permute-done.13
  43.0 0.5 pad_maximum_fusion.pad_ref
  43.5 13.6 %shard_map.113 = f32[512,256]{1,0:T(8,128)S(1)} custom-call(s32[294]{0:T(512)S(1)} %copy-done.4, f32[12,12,12,256]{3,2,1,0:T(8,128)S(1)} %pad_maximum_fusion.pad_ref, f32[512,98]{1,0:T(8,128)S(1)} %bitcast.17, f32[98,256]{1,0:T(8,128)S(1)} %copy-done.2, f32[98,256]{1,0:T(8,128)S(1)} %copy-done.3, bf16[256,256]{1,0:T(8,128)(2,1)S(1)} %copy-done.1), custom_call_target="tpu_custom_call" | custom-call | tf_op jit(solution)/shard_map/pallas_call | solution.py:98
  57.1 6.4 %collective-permute-start.19 = (f32[256]{0:T(256)S(1)}, f32[256]{0:T(256)S(1)}, u32[]{:S(2)}, u32[]{:S(2)}) collective-permute-start(f32[256]{0:T(256)S(1)} %add_add_fusion.1), channel_id=1, source_target_pairs={{0,192},{16,208},{32,224},{48,240},{64,0},{80,16},{96,32},{112,48}... | collective-permute-start | bytes 3080 | tf_op jit(solution)/shard_map/ppermute | solution.py:57
  63.5 1.0 %collective-permute-start.18 = (f32[256]{0:T(256)S(1)}, f32[256]{0:T(256)S(1)}, u32[]{:S(2)}, u32[]{:S(2)}) collective-permute-start(f32[256]{0:T(256)S(1)} %add_add_fusion.1), channel_id=1, source_target_pairs={{0,128},{16,144},{32,160},{48,176},{64,192},{80,208},{96,224},{112... | collective-permute-start | bytes 3080 | tf_op jit(solution)/shard_map/ppermute | solution.py:57
  64.5 2.8 %collective-permute-start.17 = (f32[256]{0:T(256)S(1)}, f32[256]{0:T(256)S(1)}, u32[]{:S(2)}, u32[]{:S(2)}) collective-permute-start(f32[256]{0:T(256)S(1)} %add_add_fusion.1), channel_id=1, source_target_pairs={{0,64},{16,80},{32,96},{48,112},{64,128},{80,144},{96,160},{112,17... | collective-permute-start | bytes 3080 | tf_op jit(solution)/shard_map/ppermute | solution.py:57
  67.3 1.8 %collective-permute-start.16 = (f32[2,8,8,256]{3,2,1,0:T(8,128)S(1)}, f32[2,8,8,256]{3,2,1,0:T(8,128)S(1)}, u32[]{:S(2)}, u32[]{:S(2)}) collective-permute-start(f32[2,8,8,256]{3,2,1,0:T(8,128)S(1)} %bitcast.23), channel_id=1, source_target_pairs={{16,0},{32,16},{48,32},{64,48},{80,64},{96,80},{112,96},{128,112},... | collective-permute-start | bytes 393224 | tf_op jit(solution)/shard_map/ppermute | solution.py:18
  69.1 1.8 %collective-permute-start.15 = (f32[2,8,8,256]{3,2,1,0:T(8,128)S(1)}, f32[2,8,8,256]{3,2,1,0:T(8,128)S(1)}, u32[]{:S(2)}, u32[]{:S(2)}) collective-permute-start(f32[2,8,8,256]{3,2,1,0:T(8,128)S(1)} %bitcast.22), channel_id=1, source_target_pairs={{0,16},{16,32},{32,48},{48,64},{64,80},{80,96},{96,112},{112,128},... | collective-permute-start | bytes 393224 | tf_op jit(solution)/shard_map/ppermute | solution.py:17
  70.9 0.0 collective-permute-done.19
  70.9 0.0 collective-permute-done.18
  71.0 0.0 collective-permute-done.17
  71.0 0.0 copy-done
  71.0 0.2 fusion.14
  71.2 3.4 %collective-permute-done.16 = f32[2,8,8,256]{3,2,1,0:T(8,128)S(1)} collective-permute-done((f32[2,8,8,256]{3,2,1,0:T(8,128)S(1)}, f32[2,8,8,256]{3,2,1,0:T(8,128)S(1)}, u32[]{:S(2)}, u32[]{:S(2)}) %collective-permute-start.16) | collective-permute-done | bytes 131104 | tf_op jit(solution)/shard_map/ppermute | solution.py:18
  74.6 3.1 %collective-permute-done.15 = f32[2,8,8,256]{3,2,1,0:T(8,128)S(1)} collective-permute-done((f32[2,8,8,256]{3,2,1,0:T(8,128)S(1)}, f32[2,8,8,256]{3,2,1,0:T(8,128)S(1)}, u32[]{:S(2)}, u32[]{:S(2)}) %collective-permute-start.15) | collective-permute-done | bytes 131104 | tf_op jit(solution)/shard_map/ppermute | solution.py:17
  77.7 0.1 pad_maximum_fusion.1
  77.7 0.7 fusion.9
  78.5 0.1 fusion.8
  78.5 4.3 %fusion.7 = f32[4096]{0:T(1024)} fusion(bf16[768,256]{1,0:T(8,128)(2,1)S(1)} %fusion.8, s32[4096]{0:T(1024)S(1)} %copy-done.8, bf16[4096,256]{0,1:T(8,128)(2,1)S(1)} %copy.12), kind=kOutput, calls=%fused_computation.11 | convolution fusion | flops 1616900096 | bytes 2523136 | tf_op jit(solution)/shard_map/dot_general | solution.py:145
  (16 shorter events, 0.2 us)
Async XLA Ops:
  0.6 70.4 %copy-start = (f32[256,256]{1,0:T(8,128)S(1)}, f32[256,256]{1,0:T(8,128)}, u32[]{:S(2)}) copy-start(f32[256,256]{1,0:T(8,128)} %param.22) | copy-start | bytes 786436
  0.6 3.0 %copy-start.6 = (f32[4096]{0:T(1024)S(1)}, f32[4096]{0:T(1024)}, u32[]{:S(2)}) copy-start(f32[4096]{0:T(1024)} %param.15) | copy-start | bytes 49156
  0.7 3.0 %copy-start.7 = (s32[4096]{0:T(1024)S(1)}, s32[4096]{0:T(1024)}, u32[]{:S(2)}) copy-start(s32[4096]{0:T(1024)} %param.16) | copy-start | bytes 49156
  0.7 3.0 %copy-start.8 = (s32[4096]{0:T(1024)S(1)}, s32[4096]{0:T(1024)}, u32[]{:S(2)}) copy-start(s32[4096]{0:T(1024)} %param.17) | copy-start | bytes 49156
  6.1 15.0 %collective-permute-start.9 = (f32[4,8,8,256]{3,2,1,0:T(8,128)S(1)}, f32[4,8,8,256]{3,2,1,0:T(8,128)S(1)}, u32[]{:S(2)}, u32[]{:S(2)}) collective-permute-start(f32[4,8,8,256]{3,2,1,0:T(8,128)S(1)} %bitcast.21), channel_id=1, source_target_pairs={{0,16},{16,32},{32,48},{48,64},{64,80},{80,96},{96,112},{112,128},... | collective-permute-start | bytes 786440 | tf_op jit(solution)/shard_map/ppermute | solution.py:130
  9.4 14.9 %collective-permute-start.10 = (f32[4,8,8,256]{3,2,1,0:T(8,128)S(1)}, f32[4,8,8,256]{3,2,1,0:T(8,128)S(1)}, u32[]{:S(2)}, u32[]{:S(2)}) collective-permute-start(f32[4,8,8,256]{3,2,1,0:T(8,128)S(1)} %bitcast.19), channel_id=1, source_target_pairs={{16,0},{32,16},{48,32},{64,48},{80,64},{96,80},{112,96},{128,112},... | collective-permute-start | bytes 786440 | tf_op jit(solution)/shard_map/ppermute | solution.py:131
  15.3 23.7 %copy-start.5 = (s32[8,8,8,98]{3,2,1,0:T(8,128)S(1)}, s32[8,8,8,98]{3,2,1,0:T(8,128)}, u32[]{:S(2)}) copy-start(s32[8,8,8,98]{3,2,1,0:T(8,128)} %param.18) | copy-start | bytes 602116
  15.3 9.7 %collective-permute-start.2 = (f32[256]{0:T(256)S(1)}, f32[256]{0:T(256)S(1)}, u32[]{:S(2)}, u32[]{:S(2)}) collective-permute-start(f32[256]{0:T(256)S(1)} %convert_reduce_fusion), channel_id=1, source_target_pairs={{0,3},{1,0},{2,1},{3,2},{4,7},{5,4},{6,5},{7,6},{8,11},{9,8},{10,9... | collective-permute-start | bytes 3080 | tf_op jit(solution)/shard_map/ppermute | solution.py:57
  16.2 8.8 %collective-permute-start.1 = (f32[256]{0:T(256)S(1)}, f32[256]{0:T(256)S(1)}, u32[]{:S(2)}, u32[]{:S(2)}) collective-permute-start(f32[256]{0:T(256)S(1)} %convert_reduce_fusion), channel_id=1, source_target_pairs={{0,2},{1,3},{2,0},{3,1},{4,6},{5,7},{6,4},{7,5},{8,10},{9,11},{10,... | collective-permute-start | bytes 3080 | tf_op jit(solution)/shard_map/ppermute | solution.py:57
  17.3 7.7 %collective-permute-start = (f32[256]{0:T(256)S(1)}, f32[256]{0:T(256)S(1)}, u32[]{:S(2)}, u32[]{:S(2)}) collective-permute-start(f32[256]{0:T(256)S(1)} %convert_reduce_fusion), channel_id=1, source_target_pairs={{0,1},{1,2},{2,3},{3,0},{4,5},{5,6},{6,7},{7,4},{8,9},{9,10},{10,1... | collective-permute-start | bytes 3080 | tf_op jit(solution)/shard_map/ppermute | solution.py:57
  24.4 5.2 %collective-permute-start.12 = (f32[12,2,8,256]{3,2,1,0:T(8,128)S(1)}, f32[12,2,8,256]{3,2,1,0:T(8,128)S(1)}, u32[]{:S(2)}, u32[]{:S(2)}) collective-permute-start(f32[12,2,8,256]{3,2,1,0:T(8,128)S(1)} %get-tuple-element.33), channel_id=1, source_target_pairs={{4,0},{8,4},{12,8},{0,12},{5,1},{9,5},{13,9},{1,13},{6,2},{10,6},{... | collective-permute-start | bytes 589832 | tf_op jit(solution)/shard_map/ppermute | solution.py:18
  24.5 6.4 %collective-permute-start.11 = (f32[12,2,8,256]{3,2,1,0:T(8,128)S(1)}, f32[12,2,8,256]{3,2,1,0:T(8,128)S(1)}, u32[]{:S(2)}, u32[]{:S(2)}) collective-permute-start(f32[12,2,8,256]{3,2,1,0:T(8,128)S(1)} %get-tuple-element.32), channel_id=1, source_target_pairs={{0,4},{4,8},{8,12},{12,0},{1,5},{5,9},{9,13},{13,1},{2,6},{6,10},{... | collective-permute-start | bytes 589832 | tf_op jit(solution)/shard_map/ppermute | solution.py:17
  25.0 9.5 %collective-permute-start.5 = (f32[256]{0:T(256)S(1)}, f32[256]{0:T(256)S(1)}, u32[]{:S(2)}, u32[]{:S(2)}) collective-permute-start(f32[256]{0:T(256)S(1)} %add_add_fusion.3), channel_id=1, source_target_pairs={{0,12},{4,0},{8,4},{12,8},{1,13},{5,1},{9,5},{13,9},{2,14},{6,2},{... | collective-permute-start | bytes 3080 | tf_op jit(solution)/shard_map/ppermute | solution.py:57
  26.4 8.1 %collective-permute-start.4 = (f32[256]{0:T(256)S(1)}, f32[256]{0:T(256)S(1)}, u32[]{:S(2)}, u32[]{:S(2)}) collective-permute-start(f32[256]{0:T(256)S(1)} %add_add_fusion.3), channel_id=1, source_target_pairs={{0,8},{4,12},{8,0},{12,4},{1,9},{5,13},{9,1},{13,5},{2,10},{6,14},... | collective-permute-start | bytes 3080 | tf_op jit(solution)/shard_map/ppermute | solution.py:57
  27.1 7.4 %collective-permute-start.3 = (f32[256]{0:T(256)S(1)}, f32[256]{0:T(256)S(1)}, u32[]{:S(2)}, u32[]{:S(2)}) collective-permute-start(f32[256]{0:T(256)S(1)} %add_add_fusion.3), channel_id=1, source_target_pairs={{0,4},{4,8},{8,12},{12,0},{1,5},{5,9},{9,13},{13,1},{2,6},{6,10},{... | collective-permute-start | bytes 3080 | tf_op jit(solution)/shard_map/ppermute | solution.py:57
  31.1 12.3 %copy-start.1 = (bf16[256,256]{1,0:T(8,128)(2,1)S(1)}, bf16[256,256]{1,0:T(8,128)(2,1)}, u32[]{:S(2)}) copy-start(bf16[256,256]{1,0:T(8,128)(2,1)} %base_ref.1) | copy-start | bytes 393220
  31.1 12.3 %copy-start.2 = (f32[98,256]{1,0:T(8,128)S(1)}, f32[98,256]{1,0:T(8,128)}, u32[]{:S(2)}) copy-start(f32[98,256]{1,0:T(8,128)} %rs_ref.1) | copy-start | bytes 301060
  31.1 12.3 %copy-start.3 = (f32[98,256]{1,0:T(8,128)S(1)}, f32[98,256]{1,0:T(8,128)}, u32[]{:S(2)}) copy-start(f32[98,256]{1,0:T(8,128)} %cs_ref.1) | copy-start | bytes 301060
  31.1 12.3 %copy-start.4 = (s32[294]{0:T(512)S(1)}, s32[294]{0:T(512)}, u32[]{:S(2)}) copy-start(s32[294]{0:T(512)} %constant.59.clone.tab_ref) | copy-start | bytes 3532
  31.1 11.8 %collective-permute-start.14 = (f32[12,12,2,256]{3,2,1,0:T(2,128)S(1)}, f32[12,12,2,256]{3,2,1,0:T(2,128)S(1)}, u32[]{:S(2)}, u32[]{:S(2)}) collective-permute-start(f32[12,12,2,256]{3,2,1,0:T(2,128)S(1)} %get-tuple-element.31), channel_id=1, source_target_pairs={{1,0},{2,1},{3,2},{0,3},{5,4},{6,5},{7,6},{4,7},{9,8},{10,9},{11,1... | collective-permute-start | bytes 884744 | tf_op jit(solution)/shard_map/ppermute | solution.py:18
  32.1 10.9 %collective-permute-start.13 = (f32[12,12,2,256]{3,2,1,0:T(2,128)S(1)}, f32[12,12,2,256]{3,2,1,0:T(2,128)S(1)}, u32[]{:S(2)}, u32[]{:S(2)}) collective-permute-start(f32[12,12,2,256]{3,2,1,0:T(2,128)S(1)} %get-tuple-element.30), channel_id=1, source_target_pairs={{0,1},{1,2},{2,3},{3,0},{4,5},{5,6},{6,7},{7,4},{8,9},{9,10},{10,1... | collective-permute-start | bytes 884744 | tf_op jit(solution)/shard_map/ppermute | solution.py:17
  34.5 5.2 %collective-permute-start.8 = (f32[256]{0:T(256)S(1)}, f32[256]{0:T(256)S(1)}, u32[]{:S(2)}, u32[]{:S(2)}) collective-permute-start(f32[256]{0:T(256)S(1)} %add_add_fusion.2), channel_id=1, source_target_pairs={{0,48},{16,0},{32,16},{48,32},{64,112},{80,64},{96,80},{112,96},{1... | collective-permute-start | bytes 3080 | tf_op jit(solution)/shard_map/ppermute | solution.py:57
  36.9 3.6 %collective-permute-start.7 = (f32[256]{0:T(256)S(1)}, f32[256]{0:T(256)S(1)}, u32[]{:S(2)}, u32[]{:S(2)}) collective-permute-start(f32[256]{0:T(256)S(1)} %add_add_fusion.2), channel_id=1, source_target_pairs={{0,32},{16,48},{32,0},{48,16},{64,96},{80,112},{96,64},{112,80},{1... | collective-permute-start | bytes 3080 | tf_op jit(solution)/shard_map/ppermute | solution.py:57
  37.0 6.0 %collective-permute-start.6 = (f32[256]{0:T(256)S(1)}, f32[256]{0:T(256)S(1)}, u32[]{:S(2)}, u32[]{:S(2)}) collective-permute-start(f32[256]{0:T(256)S(1)} %add_add_fusion.2), channel_id=1, source_target_pairs={{0,16},{16,32},{32,48},{48,0},{64,80},{80,96},{96,112},{112,64},{1... | collective-permute-start | bytes 3080 | tf_op jit(solution)/shard_map/ppermute | solution.py:57
  57.1 13.8 %collective-permute-start.19 = (f32[256]{0:T(256)S(1)}, f32[256]{0:T(256)S(1)}, u32[]{:S(2)}, u32[]{:S(2)}) collective-permute-start(f32[256]{0:T(256)S(1)} %add_add_fusion.1), channel_id=1, source_target_pairs={{0,192},{16,208},{32,224},{48,240},{64,0},{80,16},{96,32},{112,48}... | collective-permute-start | bytes 3080 | tf_op jit(solution)/shard_map/ppermute | solution.py:57
  63.5 7.5 %collective-permute-start.18 = (f32[256]{0:T(256)S(1)}, f32[256]{0:T(256)S(1)}, u32[]{:S(2)}, u32[]{:S(2)}) collective-permute-start(f32[256]{0:T(256)S(1)} %add_add_fusion.1), channel_id=1, source_target_pairs={{0,128},{16,144},{32,160},{48,176},{64,192},{80,208},{96,224},{112... | collective-permute-start | bytes 3080 | tf_op jit(solution)/shard_map/ppermute | solution.py:57
  64.5 6.5 %collective-permute-start.17 = (f32[256]{0:T(256)S(1)}, f32[256]{0:T(256)S(1)}, u32[]{:S(2)}, u32[]{:S(2)}) collective-permute-start(f32[256]{0:T(256)S(1)} %add_add_fusion.1), channel_id=1, source_target_pairs={{0,64},{16,80},{32,96},{48,112},{64,128},{80,144},{96,160},{112,17... | collective-permute-start | bytes 3080 | tf_op jit(solution)/shard_map/ppermute | solution.py:57
  67.3 7.3 %collective-permute-start.16 = (f32[2,8,8,256]{3,2,1,0:T(8,128)S(1)}, f32[2,8,8,256]{3,2,1,0:T(8,128)S(1)}, u32[]{:S(2)}, u32[]{:S(2)}) collective-permute-start(f32[2,8,8,256]{3,2,1,0:T(8,128)S(1)} %bitcast.23), channel_id=1, source_target_pairs={{16,0},{32,16},{48,32},{64,48},{80,64},{96,80},{112,96},{128,112},... | collective-permute-start | bytes 393224 | tf_op jit(solution)/shard_map/ppermute | solution.py:18
  69.1 8.6 %collective-permute-start.15 = (f32[2,8,8,256]{3,2,1,0:T(8,128)S(1)}, f32[2,8,8,256]{3,2,1,0:T(8,128)S(1)}, u32[]{:S(2)}, u32[]{:S(2)}) collective-permute-start(f32[2,8,8,256]{3,2,1,0:T(8,128)S(1)} %bitcast.22), channel_id=1, source_target_pairs={{0,16},{16,32},{32,48},{48,64},{64,80},{80,96},{96,112},{112,128},... | collective-permute-start | bytes 393224 | tf_op jit(solution)/shard_map/ppermute | solution.py:17
